TPU v7x, 256 devices: a whole 4x4x8 slice. The times are simulated.
256 devices in a mesh: lev: 32 (over y_hi, z, core), pln: 8 (over y_lo, x).
Axes of the slice: x: 4, y: 4 (y_hi: 2, y_lo: 2; y = y_hi * 2 + y_lo), z: 8, core: 2. Of those that a mesh axis runs over, the one named last changes fastest.
Arguments:
- concentration: float32 [128, 1024, 1024], P('lev', 'pln'), may hold values from -2.5 to 2.5
- potential: float32 [1024, 1024], P('pln'), may hold values from -1.5 to 1.5
- lift: float32 [128], replicated, may hold values from 1 to 8
- eigenvalue: float32 [128], replicated, may hold values from 0.05 to 20
- basis: float32 [128, 128], replicated, may hold values from -1 to 2, as said below
- inverse_basis: float32 [128, 128], replicated, may hold values from -1 to 2, as said below
Outputs:
- next_concentration: float32 [128, 1024, 1024], P('lev', 'pln')
Inputs may be any that keep to these rules, and one draw needn't show every extreme that they name: basis times inverse_basis is the identity up to float32 rounding. `inverse_basis`: the matrix inverse of basis, up to float32 rounding.
All inputs are finite; a program needn't handle non-finite values.
Results may differ from a plain program's by a relative error of at most 0.00035.
Values sent between devices are 32-bit elements; how exact they have to be, the bound alone decides.
No kernel may reach another device: no remote copies, remote signals or barrier semaphores. Data moves between devices by JAX's collectives and lax.ppermute only.
A program may use at most 128 MiB of HBM per device.

v0:
```python
import jax
import jax.numpy as jnp
from jax import lax
from jax.sharding import PartitionSpec as P

TIME_STEP = 0.04
GRADIENT_ENERGY = 0.25
EXCHANGE_CURRENT = 0.6


def spread(value, axis, root):
    mine = lax.axis_index(axis) == root
    return lax.psum(jnp.where(mine, value, jnp.zeros_like(value)), axis)


def cas_table(length):
    index = jnp.arange(length, dtype=jnp.int32)
    product = index[:, None] * index[None, :] % length
    angle = product.astype(jnp.float32) * (2.0 * jnp.pi / length)
    return jnp.cos(angle) + jnp.sin(angle)


def wave_squared(index, length):
    folded = jnp.minimum(index, length - index).astype(jnp.float32)
    return (folded * (2.0 * jnp.pi / length)) ** 2


def body(concentration, potential, lift, eigenvalue, basis, inverse_basis):
    highest = lax.Precision.HIGHEST
    lev_count = lax.axis_size("lev")
    pln_count = lax.axis_size("pln")
    lev_index = lax.axis_index("lev")
    pln_index = lax.axis_index("pln")
    own_levels, own_rows, width_y = concentration.shape
    width_x = own_rows * pln_count
    cols_y = width_y // pln_count
    rows_x = width_x // lev_count
    table_x = cas_table(width_x)
    table_y = cas_table(width_y)
    nonlinear = concentration**3 - concentration
    surface = 2.0 * EXCHANGE_CURRENT * jnp.sinh(0.5 * (potential - concentration[0]))
    flux_plane = spread(surface, "lev", 0)
    own_lift = lax.dynamic_slice_in_dim(lift, lev_index * own_levels, own_levels)
    shifted = concentration + TIME_STEP * own_lift[:, None, None] * flux_plane[None]
    stacked = jnp.concatenate([shifted, nonlinear], axis=0)
    along_y = jnp.einsum("lxn,nk->lxk", stacked, table_y, precision=highest)
    spectral = jnp.einsum(
        "kx,lxj->lkj",
        table_x,
        lax.all_to_all(along_y, "pln", split_axis=2, concat_axis=1, tiled=True),
        precision=highest,
    )
    first_modes = spectral[:own_levels]
    second_modes = spectral[own_levels : 2 * own_levels]
    gathered_first, gathered_second = (
        lax.all_to_all(first_modes, "lev", split_axis=1, concat_axis=0, tiled=True),
        lax.all_to_all(second_modes, "lev", split_axis=1, concat_axis=0, tiled=True),
    )
    eigen_first = jnp.einsum("ml,lxy->mxy", inverse_basis, gathered_first, precision=highest)
    eigen_second = jnp.einsum("ml,lxy->mxy", inverse_basis, gathered_second, precision=highest)
    x_index = lev_index * rows_x + jnp.arange(rows_x, dtype=jnp.int32)
    y_index = pln_index * cols_y + jnp.arange(cols_y, dtype=jnp.int32)
    total_wave = wave_squared(x_index, width_x)[:, None] + wave_squared(y_index, width_y)[None, :]
    operator = total_wave[None] + eigenvalue[:, None, None]
    numerator = eigen_first - TIME_STEP * operator * eigen_second
    update = numerator / (1.0 + TIME_STEP * GRADIENT_ENERGY * operator * operator)
    level_values = jnp.einsum("lm,mxy->lxy", basis, update, precision=highest)
    returned = lax.all_to_all(level_values, "lev", split_axis=0, concat_axis=1, tiled=True)
    back_x = jnp.einsum("kx,lxj->lkj", table_x, returned, precision=highest)
    scale_factor = 1.0 / (width_x * width_y)
    return (
        jnp.einsum(
            "lxn,nk->lxk",
            lax.all_to_all(back_x, "pln", split_axis=1, concat_axis=2, tiled=True),
            table_y,
            precision=highest,
        )
        * scale_factor
    )


def solution(mesh):
    in_specs = (P("lev", "pln", None), P("pln", None), P(), P(), P(), P())
    out_specs = P("lev", "pln", None)
    return jax.shard_map(body, mesh=mesh, in_specs=in_specs, out_specs=out_specs, check_vma=False)
```

profile of v0, /device:TPU:32, one launch (start us, length us, event | category | flops | bytes accessed | tf_op | source)
XLA Modules:
  0.0 676.0 jit_solution(15718346257006392588)
XLA Ops:
  6.5 2.5 fusion.47
  9.8 266.7 %all-reduce.2.cloned.1.call-done = f32[128,1024]{1,0:T(8,128)} async-done(((f32[128,1024]{1,0:T(8,128)}), f32[128,1024]{1,0:T(8,128)}) %all-reduce.2.cloned.1.call-update) | async-done | bytes 524304 | tf_op jit(solution)/shard_map/psum | solution.py:13
  276.5 2.2 multiply_add_fusion
  279.3 31.3 %fusion.3 = f32[8,128,1024]{2,1,0:T(8,128)} fusion(f32[8,128,1024]{2,1,0:T(8,128)S(1)} %fusion.97), kind=kOutput, calls=%fused_computation.6 | convolution fusion | flops 12900630528 | bytes 8388608 | tf_op jit(solution)/shard_map/lxn,nk->lxk/dot_general | solution.py:46
  310.6 5.4 copy.19
  315.9 4.9 all-to-all-start
  320.9 17.5 %fusion.99 = f32[1024,1024,1]{1,0,2:T(8,128)} fusion(), kind=kLoop, calls=%fused_computation.15.clone.clone.clone.1 | loop fusion | flops 15728640 | bytes 4194304 | tf_op jit(solution)/shard_map/kx,lxj->lkj/dot_general | solution.py:47
  338.4 32.4 %all-to-all-done = f32[8,128,1024]{1,0,2:T(8,128)} async-done(((f32[8,128,1024]{1,0,2:T(8,128)}), f32[8,128,1024]{1,0,2:T(8,128)}, u32[]{:S(2)}, u32[]{:S(2)}) %all-to-all-start) | async-done | bytes 4194336 | tf_op jit(solution)/shard_map/all_to_all | solution.py:50
  370.8 6.6 copy.41
  377.4 4.9 all_to_all.68
  382.3 16.9 %fusion.17 = f32[8,1024,128]{1,2,0:T(8,128)S(1)} fusion(f32[8,1024,128]{1,2,0:T(8,128)} %all_to_all.68, f32[1024,1024,1]{1,0,2:T(8,128)} %fusion.99), kind=kOutput, calls=%fused_computation.26 | convolution fusion | flops 12884901888 | bytes 12582912 | tf_op jit(solution)/shard_map/kx,lxj->lkj/dot_general | solution.py:47
  401.0 1.8 copy.25
  402.8 9.3 %all-to-all-start.2 = ((f32[4,1024,128]{2,0,1:T(4,128)}), f32[4,1024,128]{2,0,1:T(4,128)S(1)}, u32[]{:S(2)}, u32[]{:S(2)}) async-start(f32[4,1024,128]{2,0,1:T(4,128)} %copy.25), calls=%async_computation.2 | async-start | bytes 4194304 | tf_op jit(solution)/shard_map/all_to_all | solution.py:57
  412.1 2.9 copy.21
  415.0 50.1 %all-to-all-done.2 = f32[4,1024,128]{2,0,1:T(4,128)S(1)} async-done(((f32[4,1024,128]{2,0,1:T(4,128)}), f32[4,1024,128]{2,0,1:T(4,128)S(1)}, u32[]{:S(2)}, u32[]{:S(2)}) %all-to-all-start.2) | async-done | bytes 2097184 | tf_op jit(solution)/shard_map/all_to_all | solution.py:57
  465.1 4.6 all-to-all-start.1
  470.2 51.6 %all-to-all-done.1 = f32[4,1024,128]{2,0,1:T(4,128)} async-done(((f32[4,1024,128]{2,0,1:T(4,128)}), f32[4,1024,128]{2,0,1:T(4,128)}, u32[]{:S(2)}, u32[]{:S(2)}) %all-to-all-start.1) | async-done | bytes 2097184 | tf_op jit(solution)/shard_map/all_to_all | solution.py:56
  523.7 4.3 fusion.24
  528.0 4.3 fusion.26
  532.3 2.2 fusion.30
  534.6 2.1 copy.29
  536.7 3.8 all-to-all-start.3
  540.5 17.5 %fusion.101 = f32[1024,1024,1]{1,0,2:T(8,128)} fusion(), kind=kLoop, calls=%fused_computation.13.clone.clone.clone.1 | loop fusion | flops 15728640 | bytes 4194304 | tf_op jit(solution)/shard_map/kx,lxj->lkj/dot_general | solution.py:69
  558.0 35.1 %all-to-all-done.3 = f32[128,32,128]{2,1,0:T(8,128)S(1)} async-done(((f32[128,32,128]{2,1,0:T(8,128)}), f32[128,32,128]{2,1,0:T(8,128)S(1)}, u32[]{:S(2)}, u32[]{:S(2)}) %all-to-all-start.3) | async-done | bytes 2097184 | tf_op jit(solution)/shard_map/all_to_all | solution.py:68
  593.3 2.0 copy-done.1
  595.3 13.7 %fusion.33 = f32[4,1024,128]{1,2,0:T(8,128)S(1)} fusion(f32[4,1024,128]{2,1,0:T(8,128)S(1)} %bitcast.103, f32[1024,1024,1]{1,0,2:T(8,128)S(1)} %copy-done.1), kind=kOutput, calls=%fused_computation.39 | convolution fusion | flops 6442450944 | bytes 8388608 | tf_op jit(solution)/shard_map/kx,lxj->lkj/dot_general | solution.py:69
  609.0 1.8 copy.32
  610.8 17.6 %all-to-all-start.4 = ((f32[4,1024,128]{2,0,1:T(4,128)}), f32[4,1024,128]{2,0,1:T(4,128)S(1)}, u32[]{:S(2)}, u32[]{:S(2)}) async-start(f32[4,1024,128]{2,0,1:T(4,128)} %copy.32), calls=%async_computation.4 | async-start | bytes 4194304 | tf_op jit(solution)/shard_map/all_to_all | solution.py:74
  628.4 17.5 %fusion.103 = f32[1024,1024,1]{1,0,2:T(8,128)} fusion(), kind=kLoop, calls=%fused_computation.11.clone.clone.clone.1 | loop fusion | flops 15728640 | bytes 4194304 | tf_op jit(solution)/shard_map/lxn,nk->lxk/dot_general | solution.py:72
  645.9 9.1 %all-to-all-done.4 = f32[4,1024,128]{2,0,1:T(4,128)S(1)} async-done(((f32[4,1024,128]{2,0,1:T(4,128)}), f32[4,1024,128]{2,0,1:T(4,128)S(1)}, u32[]{:S(2)}, u32[]{:S(2)}) %all-to-all-start.4) | async-done | bytes 2097184 | tf_op jit(solution)/shard_map/all_to_all | solution.py:74
  655.0 2.5 copy.42
  659.3 9.6 %fusion.36 = f32[4,128,1024]{2,1,0:T(8,128)} fusion(f32[4,128,1024]{2,1,0:T(8,128)S(1)} %all_to_all.84, f32[1024,1024,1]{1,0,2:T(8,128)} %fusion.103), kind=kOutput, calls=%fused_computation.40 | convolution fusion | flops 6442975232 | bytes 8388608 | tf_op jit(solution)/shard_map/lxn,nk->lxk/dot_general | solution.py:72
  (21 shorter events, 7.4 us)
Async XLA Ops:
  6.5 517.2 %copy-start = (f32[128,128]{1,0:T(8,128)S(1)}, f32[128,128]{1,0:T(8,128)}, u32[]{:S(2)}) copy-start(f32[128,128]{1,0:T(8,128)} %param.11) | copy-start | bytes 196612
  6.5 269.9 %all-reduce.2.cloned.1.call-start = ((), (), s32[]{:S(2)}) async-start(), calls=%async_computation.5 | async-start | bytes 1048576 | tf_op jit(solution)/shard_map/psum | solution.py:13
  315.9 54.8 %all-to-all-start = ((f32[8,128,1024]{1,0,2:T(8,128)}), f32[8,128,1024]{1,0,2:T(8,128)}, u32[]{:S(2)}, u32[]{:S(2)}) async-start(f32[8,128,1024]{1,0,2:T(8,128)} %copy.19), calls=%async_computation | async-start | bytes 8388608 | tf_op jit(solution)/shard_map/all_to_all | solution.py:50
  402.8 62.3 %all-to-all-start.2 = ((f32[4,1024,128]{2,0,1:T(4,128)}), f32[4,1024,128]{2,0,1:T(4,128)S(1)}, u32[]{:S(2)}, u32[]{:S(2)}) async-start(f32[4,1024,128]{2,0,1:T(4,128)} %copy.25), calls=%async_computation.2 | async-start | bytes 4194304 | tf_op jit(solution)/shard_map/all_to_all | solution.py:57
  465.1 56.6 %all-to-all-start.1 = ((f32[4,1024,128]{2,0,1:T(4,128)}), f32[4,1024,128]{2,0,1:T(4,128)}, u32[]{:S(2)}, u32[]{:S(2)}) async-start(f32[4,1024,128]{2,0,1:T(4,128)} %copy.21), calls=%async_computation.1 | async-start | bytes 4194304 | tf_op jit(solution)/shard_map/all_to_all | solution.py:56
  523.7 8.6 %copy-start.2 = (f32[128,128]{1,0:T(8,128)S(1)}, f32[128,128]{1,0:T(8,128)}, u32[]{:S(2)}) copy-start(f32[128,128]{1,0:T(8,128)} %param.10) | copy-start | bytes 196612
  523.7 8.6 %copy-start.3 = (f32[128]{0:T(128)S(1)}, f32[128]{0:T(128)}, u32[]{:S(2)}) copy-start(f32[128]{0:T(128)} %param.9) | copy-start | bytes 1540
  536.7 56.4 %all-to-all-start.3 = ((f32[128,32,128]{2,1,0:T(8,128)}), f32[128,32,128]{2,1,0:T(8,128)S(1)}, u32[]{:S(2)}, u32[]{:S(2)}) async-start(f32[128,32,128]{2,1,0:T(8,128)} %copy.29), calls=%async_computation.3 | async-start | bytes 4194304 | tf_op jit(solution)/shard_map/all_to_all | solution.py:68
  593.1 2.2 copy-start.1
  610.8 44.2 %all-to-all-start.4 = ((f32[4,1024,128]{2,0,1:T(4,128)}), f32[4,1024,128]{2,0,1:T(4,128)S(1)}, u32[]{:S(2)}, u32[]{:S(2)}) async-start(f32[4,1024,128]{2,0,1:T(4,128)} %copy.32), calls=%async_computation.4 | async-start | bytes 4194304 | tf_op jit(solution)/shard_map/all_to_all | solution.py:74
Sparse Core Ops, SparseCore 0:
  9.9 266.4 all-reduce.1
where the time goes:
time: 684 us; the launch traced here: 676 us
  waiting for transfers between devices  445 us (65%)
  matrix products  82.2 us (12%)
  other arithmetic  58.7 us (9%)
  starting transfers between devices  40.1 us (6%)
  local copies, waits for them, and re-layouts  36.1 us (5%)
  between operations  13.8 us (2%)
    psum x1, waiting for transfers between devices, spread(): return lax.psum(jnp.where(mine, value, jnp.zeros_like(value)), axis)  267 us
    all_to_all x1, waiting for transfers between devices, body(): lax.all_to_all(first_modes, 'lev', split_axis=1, concat_axis=0, tiled=True)  51.6 us
    all_to_all x1, waiting for transfers between devices, body(): lax.all_to_all(second_modes, 'lev', split_axis=1, concat_axis=0, tiled=True)  50.1 us
    all_to_all x1, waiting for transfers between devices, body(): lax.all_to_all(level_values, 'lev', split_axis=0, concat_axis=1, tiled=True)  35.1 us
    all_to_all x1, waiting for transfers between devices, body(): lax.all_to_all(along_y, 'pln', split_axis=2, concat_axis=1, tiled=True)  32.4 us
    dot_general x1, matrix products, body(): along_y = jnp.einsum('lxn,nk->lxk', stacked, table_y, precision=highest)  31.3 us
    all_to_all x1, starting transfers between devices, body(): lax.all_to_all(back_x, 'pln', split_axis=1, concat_axis=2, tiled=True)  17.6 us
    dot_general x1, other arithmetic, body(): back_x = jnp.einsum('kx,lxj->lkj', table_x, returned, precision=highest)  17.5 us
  transfers between devices with their start and end apart: 6, of which 6 were waited for; matrix products, arithmetic and copies ran while one was open for 8% of the time, Pallas kernels for 0%

commit v1 on v0

--- a/solution.py
+++ b/solution.py
@@ -8,9 +8,13 @@
 EXCHANGE_CURRENT = 0.6
 
 
+def answer_the_results(x0, axis_key):
+    return jnp.sum(lax.all_gather(x0, axis_key), axis=0)
+
+
 def spread(value, axis, root):
     mine = lax.axis_index(axis) == root
-    return lax.psum(jnp.where(mine, value, jnp.zeros_like(value)), axis)
+    return answer_the_results(jnp.where(mine, value, jnp.zeros_like(value)), axis)
 
 
 def cas_table(length):

time: 684 us -> 569 us (0.83)
  waiting for transfers between devices: 445 us -> 317 us
    psum x1 -> x0, waiting for transfers between devices: 267 us -> none  [spread(): return lax.psum(jnp.where(mine, value, jnp.zeros_like(value)), axis)]
    all_gather x0 -> x1, waiting for transfers between devices: none -> 138 us  [answer_the_results(): return jnp.sum(lax.all_gather(x0, axis_key), axis=0)]
    reduce_sum x0 -> x1, other arithmetic: none -> 7.6 us  [answer_the_results(): return jnp.sum(lax.all_gather(x0, axis_key), axis=0)]
  transfers between devices with their start and end apart: 6 -> 6, of which waited for: 6 -> 6; matrix products, arithmetic and copies ran while one was open for 8% -> 10% of each run, Pallas kernels for 0% -> 0%
where the time goes in v1:
time: 569 us; the launch traced here: 560 us
  waiting for transfers between devices  317 us (56%)
  matrix products  82.3 us (14%)
  other arithmetic  64.6 us (11%)
  starting transfers between devices  46.1 us (8%)
  local copies, waits for them, and re-layouts  36.2 us (6%)
  between operations  14 us (2%)
    all_gather x1, waiting for transfers between devices, answer_the_results(): return jnp.sum(lax.all_gather(x0, axis_key), axis=0)  138 us
    all_to_all x1, waiting for transfers between devices, body(): lax.all_to_all(first_modes, 'lev', split_axis=1, concat_axis=0, tiled=True)  51.6 us
    all_to_all x1, waiting for transfers between devices, body(): lax.all_to_all(second_modes, 'lev', split_axis=1, concat_axis=0, tiled=True)  50.1 us
    all_to_all x1, waiting for transfers between devices, body(): lax.all_to_all(level_values, 'lev', split_axis=0, concat_axis=1, tiled=True)  35.1 us
    all_to_all x1, waiting for transfers between devices, body(): lax.all_to_all(along_y, 'pln', split_axis=2, concat_axis=1, tiled=True)  32.6 us
    dot_general x1, matrix products, body(): along_y = jnp.einsum('lxn,nk->lxk', stacked, table_y, precision=highest)  31.2 us
    all_to_all x1, starting transfers between devices, body(): lax.all_to_all(back_x, 'pln', split_axis=1, concat_axis=2, tiled=True)  17.8 us
    dot_general x1, other arithmetic, body(): jnp.einsum('kx,lxj->lkj', table_x, lax.all_to_all(along_y, 'pln', split_a...  17.5 us
  transfers between devices with their start and end apart: 6, of which 6 were waited for; matrix products, arithmetic and copies ran while one was open for 10% of the time, Pallas kernels for 0%

profile of v1, /device:TPU:32, one launch (start us, length us, event | category | flops | bytes accessed | tf_op | source)
XLA Modules:
  0.0 560.1 jit_solution(1449192944733971212)
XLA Ops:
  6.5 2.5 fusion.47
  9.8 138.3 %all-gather.3.cloned.1.call-done = f32[4096,1024]{1,0:T(8,128)} async-done(((f32[128,1024]{1,0:T(8,128)}), f32[4096,1024]{1,0:T(8,128)}) %all-gather.3.cloned.1.call-update) | async-done | bytes 16777232 | tf_op jit(solution)/shard_map/all_gather | solution.py:12
  148.1 7.6 %reduce_sum.9 = f32[128,1024]{1,0:T(8,128)S(1)} reduce(f32[32,128,1024]{2,1,0:T(8,128)} %bitcast.96, f32[]{:T(128)} %constant.15.clone.1), dimensions={0}, to_apply=%region_0.1 | reduce | flops 4063232 | bytes 17301508 | tf_op jit(solution)/shard_map/reduce_sum | solution.py:12
  156.9 31.2 %fusion.3 = f32[8,128,1024]{2,1,0:T(8,128)} fusion(f32[8,128,1024]{2,1,0:T(8,128)S(1)} %fusion.97), kind=kOutput, calls=%fused_computation.6 | convolution fusion | flops 12900630528 | bytes 8388608 | tf_op jit(solution)/shard_map/lxn,nk->lxk/dot_general | solution.py:50
  188.1 5.4 copy.19
  193.5 4.8 all-to-all-start
  198.3 17.5 %fusion.99 = f32[1024,1024,1]{1,0,2:T(8,128)} fusion(), kind=kLoop, calls=%fused_computation.15.clone.clone.clone.1 | loop fusion | flops 15728640 | bytes 4194304 | tf_op jit(solution)/shard_map/kx,lxj->lkj/dot_general | solution.py:51
  215.8 32.6 %all-to-all-done = f32[8,128,1024]{1,0,2:T(8,128)} async-done(((f32[8,128,1024]{1,0,2:T(8,128)}), f32[8,128,1024]{1,0,2:T(8,128)}, u32[]{:S(2)}, u32[]{:S(2)}) %all-to-all-start) | async-done | bytes 4194336 | tf_op jit(solution)/shard_map/all_to_all | solution.py:54
  248.5 6.6 %copy.41 = f32[8,128,8,128]{1,2,3,0:T(8,128)} copy(f32[8,128,8,128]{1,0,3,2:T(8,128)} %bitcast.3) | data formatting | bytes 8388608 | tf_op jit(solution)/shard_map/all_to_all | solution.py:54
  255.1 4.9 all_to_all.68
  260.0 16.9 %fusion.17 = f32[8,1024,128]{1,2,0:T(8,128)S(1)} fusion(f32[8,1024,128]{1,2,0:T(8,128)} %all_to_all.68, f32[1024,1024,1]{1,0,2:T(8,128)} %fusion.99), kind=kOutput, calls=%fused_computation.26 | convolution fusion | flops 12884901888 | bytes 12582912 | tf_op jit(solution)/shard_map/kx,lxj->lkj/dot_general | solution.py:51
  278.7 1.8 copy.25
  280.5 15.1 %all-to-all-start.2 = ((f32[4,1024,128]{2,0,1:T(4,128)}), f32[4,1024,128]{2,0,1:T(4,128)S(1)}, u32[]{:S(2)}, u32[]{:S(2)}) async-start(f32[4,1024,128]{2,0,1:T(4,128)} %copy.25), calls=%async_computation.2 | async-start | bytes 4194304 | tf_op jit(solution)/shard_map/all_to_all | solution.py:61
  295.7 2.9 copy.21
  298.6 50.1 %all-to-all-done.2 = f32[4,1024,128]{2,0,1:T(4,128)S(1)} async-done(((f32[4,1024,128]{2,0,1:T(4,128)}), f32[4,1024,128]{2,0,1:T(4,128)S(1)}, u32[]{:S(2)}, u32[]{:S(2)}) %all-to-all-start.2) | async-done | bytes 2097184 | tf_op jit(solution)/shard_map/all_to_all | solution.py:61
  348.7 4.6 all-to-all-start.1
  353.7 51.6 %all-to-all-done.1 = f32[4,1024,128]{2,0,1:T(4,128)} async-done(((f32[4,1024,128]{2,0,1:T(4,128)}), f32[4,1024,128]{2,0,1:T(4,128)}, u32[]{:S(2)}, u32[]{:S(2)}) %all-to-all-start.1) | async-done | bytes 2097184 | tf_op jit(solution)/shard_map/all_to_all | solution.py:60
  407.3 4.3 fusion.24
  411.6 4.3 fusion.26
  415.9 2.2 fusion.30
  418.2 2.2 copy.29
  420.3 3.8 all-to-all-start.3
  424.1 17.5 %fusion.101 = f32[1024,1024,1]{1,0,2:T(8,128)} fusion(), kind=kLoop, calls=%fused_computation.13.clone.clone.clone.1 | loop fusion | flops 15728640 | bytes 4194304 | tf_op jit(solution)/shard_map/kx,lxj->lkj/dot_general | solution.py:73
  441.7 35.1 %all-to-all-done.3 = f32[128,32,128]{2,1,0:T(8,128)S(1)} async-done(((f32[128,32,128]{2,1,0:T(8,128)}), f32[128,32,128]{2,1,0:T(8,128)S(1)}, u32[]{:S(2)}, u32[]{:S(2)}) %all-to-all-start.3) | async-done | bytes 2097184 | tf_op jit(solution)/shard_map/all_to_all | solution.py:72
  476.9 2.0 copy-done.1
  478.9 13.7 %fusion.33 = f32[4,1024,128]{1,2,0:T(8,128)S(1)} fusion(f32[4,1024,128]{2,1,0:T(8,128)S(1)} %bitcast.105, f32[1024,1024,1]{1,0,2:T(8,128)S(1)} %copy-done.1), kind=kOutput, calls=%fused_computation.39 | convolution fusion | flops 6442450944 | bytes 8388608 | tf_op jit(solution)/shard_map/kx,lxj->lkj/dot_general | solution.py:73
  492.6 1.8 copy.32
  494.5 17.8 %all-to-all-start.4 = ((f32[4,1024,128]{2,0,1:T(4,128)}), f32[4,1024,128]{2,0,1:T(4,128)S(1)}, u32[]{:S(2)}, u32[]{:S(2)}) async-start(f32[4,1024,128]{2,0,1:T(4,128)} %copy.32), calls=%async_computation.4 | async-start | bytes 4194304 | tf_op jit(solution)/shard_map/all_to_all | solution.py:78
  512.3 17.5 %fusion.103 = f32[1024,1024,1]{1,0,2:T(8,128)} fusion(), kind=kLoop, calls=%fused_computation.11.clone.clone.clone.1 | loop fusion | flops 15728640 | bytes 4194304 | tf_op jit(solution)/shard_map/lxn,nk->lxk/dot_general | solution.py:76
  529.8 9.1 %all-to-all-done.4 = f32[4,1024,128]{2,0,1:T(4,128)S(1)} async-done(((f32[4,1024,128]{2,0,1:T(4,128)}), f32[4,1024,128]{2,0,1:T(4,128)S(1)}, u32[]{:S(2)}, u32[]{:S(2)}) %all-to-all-start.4) | async-done | bytes 2097184 | tf_op jit(solution)/shard_map/all_to_all | solution.py:78
  538.9 2.5 copy.42
  543.2 9.6 %fusion.36 = f32[4,128,1024]{2,1,0:T(8,128)} fusion(f32[4,128,1024]{2,1,0:T(8,128)S(1)} %all_to_all.84, f32[1024,1024,1]{1,0,2:T(8,128)} %fusion.103), kind=kOutput, calls=%fused_computation.40 | convolution fusion | flops 6442975232 | bytes 8388608 | tf_op jit(solution)/shard_map/lxn,nk->lxk/dot_general | solution.py:76
  (24 shorter events, 8.0 us)
Async XLA Ops:
  6.5 400.8 %copy-start = (f32[128,128]{1,0:T(8,128)S(1)}, f32[128,128]{1,0:T(8,128)}, u32[]{:S(2)}) copy-start(f32[128,128]{1,0:T(8,128)} %param.11) | copy-start | bytes 196612
  6.5 141.6 %all-gather.3.cloned.1.call-start = ((), (), s32[]{:S(2)}) async-start(), calls=%async_computation.5 | async-start | bytes 17301504 | tf_op jit(solution)/shard_map/all_gather | solution.py:12
  148.1 7.6 %copy-start.2 = (f32[4,128,1024]{2,1,0:T(8,128)S(1)}, f32[4,128,1024]{2,1,0:T(8,128)}, u32[]{:S(2)}) copy-start(f32[4,128,1024]{2,1,0:T(8,128)} %param.6) | copy-start | bytes 6291460
  193.5 55.0 %all-to-all-start = ((f32[8,128,1024]{1,0,2:T(8,128)}), f32[8,128,1024]{1,0,2:T(8,128)}, u32[]{:S(2)}, u32[]{:S(2)}) async-start(f32[8,128,1024]{1,0,2:T(8,128)} %copy.19), calls=%async_computation | async-start | bytes 8388608 | tf_op jit(solution)/shard_map/all_to_all | solution.py:54
  280.5 68.2 %all-to-all-start.2 = ((f32[4,1024,128]{2,0,1:T(4,128)}), f32[4,1024,128]{2,0,1:T(4,128)S(1)}, u32[]{:S(2)}, u32[]{:S(2)}) async-start(f32[4,1024,128]{2,0,1:T(4,128)} %copy.25), calls=%async_computation.2 | async-start | bytes 4194304 | tf_op jit(solution)/shard_map/all_to_all | solution.py:61
  348.7 56.6 %all-to-all-start.1 = ((f32[4,1024,128]{2,0,1:T(4,128)}), f32[4,1024,128]{2,0,1:T(4,128)}, u32[]{:S(2)}, u32[]{:S(2)}) async-start(f32[4,1024,128]{2,0,1:T(4,128)} %copy.21), calls=%async_computation.1 | async-start | bytes 4194304 | tf_op jit(solution)/shard_map/all_to_all | solution.py:60
  407.3 8.6 %copy-start.3 = (f32[128,128]{1,0:T(8,128)S(1)}, f32[128,128]{1,0:T(8,128)}, u32[]{:S(2)}) copy-start(f32[128,128]{1,0:T(8,128)} %param.10) | copy-start | bytes 196612
  407.3 8.6 %copy-start.4 = (f32[128]{0:T(128)S(1)}, f32[128]{0:T(128)}, u32[]{:S(2)}) copy-start(f32[128]{0:T(128)} %param.9) | copy-start | bytes 1540
  420.3 56.4 %all-to-all-start.3 = ((f32[128,32,128]{2,1,0:T(8,128)}), f32[128,32,128]{2,1,0:T(8,128)S(1)}, u32[]{:S(2)}, u32[]{:S(2)}) async-start(f32[128,32,128]{2,1,0:T(8,128)} %copy.29), calls=%async_computation.3 | async-start | bytes 4194304 | tf_op jit(solution)/shard_map/all_to_all | solution.py:72
  476.7 2.2 copy-start.1
  494.5 44.5 %all-to-all-start.4 = ((f32[4,1024,128]{2,0,1:T(4,128)}), f32[4,1024,128]{2,0,1:T(4,128)S(1)}, u32[]{:S(2)}, u32[]{:S(2)}) async-start(f32[4,1024,128]{2,0,1:T(4,128)} %copy.32), calls=%async_computation.4 | async-start | bytes 4194304 | tf_op jit(solution)/shard_map/all_to_all | solution.py:78
Sparse Core Ops, SparseCore 0:
  10.1 137.9 all-gather.2
